TPU v7x, 128 devices: a whole 4x4x4 slice. The times are simulated.
128 devices in a mesh: gx: 8 (over z, core), gy: 16 (over y, x).
Axes of the slice: x: 4, y: 4, z: 4, core: 2. Of those that a mesh axis runs over, the one named last changes fastest.
Arguments:
- hidden_in: bfloat16 [32768, 3584], P(('gx', 'gy')), may hold values from -6 to 6
- lengths: int32 [8, 4], P('gx'), may hold values from 1 to 2048, 4096 in all within a row
- attn_norm: float32 [3584], replicated, may hold values from 0.5 to 1.5
- qkv_weight: bfloat16 [3584, 4608], P('gx', 'gy'), may hold values from -0.09375 to 0.09375
- qkv_bias: float32 [4608], replicated, may hold values from -5 to 5
Outputs:
- attn: bfloat16 [32768, 3584], P(('gx', 'gy'))
- kv_rows: bfloat16 [32768, 1024], P(('gx', 'gy'))
Inputs may be any that keep to these rules, and one draw needn't show every extreme that they name: Each row of lengths sums to 4096; the longest of each row is exactly 2048.
All inputs are finite; a program needn't handle non-finite values.
Results may differ from a plain program's by a relative error of at most 0.0035.
The roundings to bfloat16 on the way count: a program that leaves them out, or rounds other values in their place, can miss the bound.
Values may be sent and summed in bfloat16 or wider, within the bound.
No kernel may reach another device: no remote copies, remote signals or barrier semaphores. Data moves between devices by JAX's collectives and lax.ppermute only.
A program may use at most 128 MiB of HBM per device.

v0:
```python
import math
import jax
import jax.numpy as jnp
from jax import lax
from jax.sharding import PartitionSpec as P

HEADS = 28
KV_HEADS = 4
HEAD_DIM = 128
key_span = 512


def norm_rows(values, gain):
    wide = values.astype(jnp.float32)
    scale = lax.rsqrt(jnp.mean(wide * wide, axis=1, keepdims=True) + 1e-06)
    return (wide * scale * gain[None, :]).astype(jnp.bfloat16)


def segment_of(index, ends):
    return jnp.sum((ends[None, :] <= index[:, None]).astype(jnp.int32), axis=1)


def rotate(block, pos, heads):
    half = HEAD_DIM // 2
    freqs = 1000000.0 ** (-2.0 * jnp.arange(half, dtype=jnp.float32) / HEAD_DIM)
    angle = pos.astype(jnp.float32)[:, None, None] * freqs[None, None, :]
    wide = block.astype(jnp.float32).reshape(block.shape[0], heads, HEAD_DIM)
    first, second = (wide[..., :half], wide[..., half:])
    turned = jnp.concatenate(
        [
            first * jnp.cos(angle) - second * jnp.sin(angle),
            second * jnp.cos(angle) + first * jnp.sin(angle),
        ],
        axis=2,
    )
    return turned.reshape(block.shape[0], heads * HEAD_DIM).astype(jnp.bfloat16)


def project_joined(normed, weight, bias):
    grouped = lax.all_gather(normed, "gy", axis=0, tiled=True)
    summed = jnp.dot(
        grouped,
        lax.all_gather(weight, "gx", axis=0, tiled=True),
        preferred_element_type=jnp.float32,
    )
    width = weight.shape[1]
    bias_block = lax.dynamic_slice_in_dim(bias, lax.axis_index("gy") * width, width, 0)
    block_out = (summed + bias_block[None, :]).astype(jnp.bfloat16)
    return lax.all_to_all(block_out, "gy", split_axis=0, concat_axis=1, tiled=True)


def on_device(hidden_in, lengths, attn_norm, qkv_weight, qkv_bias):
    rows = hidden_in.shape[0]
    first = lax.axis_index("gy") * rows
    row_lengths = lengths[0]
    qdim = HEADS * HEAD_DIM
    kdim = KV_HEADS * HEAD_DIM
    group = HEADS // KV_HEADS
    normed = norm_rows(hidden_in, attn_norm)
    joined = project_joined(normed, qkv_weight, qkv_bias)
    ends = jnp.cumsum(row_lengths)
    tokens_here = first + jnp.arange(rows, dtype=jnp.int32)
    before = ends[None, :] <= tokens_here[:, None]
    seg_here = jnp.sum(before.astype(jnp.int32), axis=1)
    begin = jnp.sum(jnp.where(before, row_lengths[None, :], 0), axis=1)
    pos = tokens_here - begin
    queries = rotate(joined[:, :qdim], pos, HEADS).reshape(rows, KV_HEADS, group, HEAD_DIM)
    keys = rotate(joined[:, qdim : qdim + kdim], pos, KV_HEADS)
    kv_rows = jnp.concatenate([keys, joined[:, qdim + kdim :]], axis=1)
    scale = 1.0 / HEAD_DIM**0.5

    def attend(carry, piece, start):
        running, total, summed = carry
        key_count = piece.shape[0]
        key_index = start + jnp.arange(key_count, dtype=jnp.int32)
        key_seg = segment_of(key_index, ends)
        key_part = piece[:, :kdim].reshape(key_count, KV_HEADS, HEAD_DIM)
        value_part = piece[:, kdim:].reshape(key_count, KV_HEADS, HEAD_DIM)
        scores = (
            jnp.einsum("rgho,ngo->ghrn", queries, key_part, preferred_element_type=jnp.float32)
            * scale
        )
        allowed = (seg_here[:, None] == key_seg[None, :]) & (
            key_index[None, :] <= tokens_here[:, None]
        )
        newest = jnp.maximum(running, jnp.max(jnp.where(allowed, scores, -1e30), axis=3))
        shrink = jnp.exp(running - newest)
        weights = jnp.where(allowed, jnp.exp(scores - newest[..., None]), 0.0)
        total = total * shrink + jnp.sum(weights, axis=3)
        summed = summed * shrink[..., None] + jnp.einsum(
            "ghrn,ngo->ghro",
            weights.astype(jnp.bfloat16),
            value_part,
            preferred_element_type=jnp.float32,
        )
        return (newest, total, summed)

    def visit(carry, piece, start):
        return attend(carry, piece, start)

    start_state = (
        jnp.full((KV_HEADS, group, rows), -1e30, jnp.float32),
        jnp.zeros((KV_HEADS, group, rows), jnp.float32),
        jnp.zeros((KV_HEADS, group, rows, HEAD_DIM), jnp.float32),
    )
    piece = lax.all_gather(kv_rows, "gy", axis=0, tiled=True)
    length = piece.shape[0]
    span = math.gcd(length, key_span)
    stacked = piece.reshape(length // span, span, piece.shape[1])
    offsets = jnp.arange(length // span, dtype=jnp.int32) * span

    def advance(state, item):
        return (visit(state, item[0], item[1]), None)

    final_state, unused = lax.scan(advance, start_state, (stacked, offsets))
    running, total, summed = final_state
    attn = (
        jnp.transpose(summed / total[..., None], (2, 0, 1, 3))
        .reshape(rows, qdim)
        .astype(jnp.bfloat16)
    )
    return (attn, kv_rows)


def solution(mesh):
    placed = (P(("gx", "gy"), None), P("gx", None), P(), P("gx", "gy"), P())
    return jax.shard_map(
        on_device,
        mesh=mesh,
        in_specs=placed,
        out_specs=(P(("gx", "gy"), None), P(("gx", "gy"), None)),
        check_vma=False,
    )
```

profile of v0, /device:TPU:0, one launch (start us, length us, event | category | flops | bytes accessed | tf_op | source)
XLA Modules:
  0.0 595.3 jit_solution(592481126304964280)
XLA Ops:
  7.9 1.9 fusion.17
  9.9 3.2 fusion.19
  13.9 24.0 %all-gather.9.cloned.1.call-done = bf16[8,448,288]{1,2,0:T(8,128)(2,1)} async-done(((bf16[1,448,288]{1,2,0:T(8,128)(2,1)}), bf16[8,448,288]{1,2,0:T(8,128)(2,1)}) %all-gather.9.cloned.1.call-update) | async-done | bytes 2064400 | tf_op jit(solution)/shard_map/all_gather | solution.py:43
  38.0 3.0 copy.34
  41.0 3.6 reshape.172
  44.5 172.0 %all-gather.5.cloned.1.call-done = bf16[4096,3584]{1,0:T(8,128)(2,1)} async-done(((bf16[256,3584]{1,0:T(8,128)(2,1)}), bf16[4096,3584]{1,0:T(8,128)(2,1)}) %all-gather.5.cloned.1.call-update) | async-done | bytes 29360144 | tf_op jit(solution)/shard_map/all_gather | solution.py:40
  216.6 14.7 %fusion.16 = bf16[4096,288]{0,1:T(8,128)(2,1)S(1)} fusion(bf16[4096,3584]{1,0:T(8,128)(2,1)} %all-gather.5.cloned.1.call-done, bf16[3584,288]{0,1:T(8,128)(2,1)} %reshape.172, f32[288]{0:T(512)S(1)} %dynamic_slice.11), kind=kOutput, calls=%fused_computation.25 | convolution fusion | flops 8458076160 | bytes 33784960 | tf_op jit(solution)/shard_map/dot_general | solution.py:41
  233.0 5.3 all-to-all-start
  239.1 34.4 %all-to-all-done = bf16[16,256,288]{1,2,0:T(8,128)(2,1)S(1)} async-done(((bf16[16,256,288]{1,2,0:T(8,128)(2,1)}), bf16[16,256,288]{1,2,0:T(8,128)(2,1)S(1)}, u32[]{:S(2)}, u32[]{:S(2)}) %all-to-all-start) | async-done | bytes 2359328 | tf_op jit(solution)/shard_map/all_to_all | solution.py:49
  276.9 1.9 convert.19
  280.8 3.0 copy.37
  283.8 65.9 %all-gather.7.cloned.1.call-done = bf16[4096,1024]{0,1:T(8,128)(2,1)} async-done(((bf16[256,1024]{0,1:T(8,128)(2,1)}), bf16[4096,1024]{0,1:T(8,128)(2,1)}) %all-gather.7.cloned.1.call-update) | async-done | bytes 8388624 | tf_op jit(solution)/shard_map/all_gather | solution.py:106
  349.7 7.5 %copy.52 = bf16[128,8,8,512]{3,2,0,1:T(8,128)(2,1)} copy(bf16[128,8,8,512]{3,2,1,0:T(8,128)(2,1)} %bitcast.86) | data formatting | bytes 16777216 | tf_op jit(solution)/shard_map/reshape | solution.py:109
  357.2 222.0 %while.15 = (s32[]{:T(128)}, f32[4,7,256]{2,1,0:T(8,128)S(1)}, f32[4,7,256]{2,1,0:T(8,128)S(1)}, f32[4,7,256,128]{3,2,1,0:T(8,128)}, s32[256]{0:T(256)S(1)}, /*i...) while((s32[]{:T(128)}, f32[4,7,256]{2,1,0:T(8,128)S(1)}, ...), condition=%wide.region_8.9_spmd.clone, body=%wide.region_4.8_spmd.clone.sunk | while | flops 1922606336 | bytes 88814816 | solution.py:115
  360.1 6.5 %fusion.43 = (f32[4,7,256]{2,1,0:T(8,128)S(1)}, f32[4,512,256,7]{2,1,3,0:T(8,128)}) fusion(pred[256,512]{0,1:T(8,128)(4,1)S(1)} %compare_and_fusion.2, bf16[512,4,128,1]{0,2,3,1:T(8,128)(2,1)S(1)} %bitcast.80, bf16[256,4,7,128]{3,0,2,1:T(8,128)(2,1)S(1)} %get-tuple-element.270), kind=kOutput, calls=%fused_computation.3.clone.1 | convolution fusion | flops 950526976 | bytes 17199104 | tf_op jit(solution)/shard_map/while/body/eval_jaxpr/rgho,ngo->ghrn/dot_general | solution.py:80
  366.6 8.3 %fusion.44 = f32[4,7,256]{2,1,0:T(8,128)S(1)} fusion(f32[4,512,256,7]{2,1,3,0:T(8,128)} %get-tuple-element.234, f32[4,7,256]{2,1,0:T(8,128)S(1)} %select_maximum_fusion.2, pred[256,512]{0,1:T(8,128)(4,1)S(1)} %compare_and_fusion.2), kind=kLoop, calls=%fused_computation.7.clone.1 | loop fusion | flops 14672896 | bytes 14868480 | tf_op jit(solution)/shard_map/while/body/eval_jaxpr/reduce_sum | solution.py:89
  375.0 8.0 %fusion.46 = f32[4,7,256,128]{3,2,1,0:T(8,128)S(1)} fusion(f32[4,7,256,128]{3,2,1,0:T(8,128)S(1)} %copy-done.1, bf16[512,4,128,1]{0,2,3,1:T(8,128)(2,1)S(1)} %bitcast.82, f32[4,512,256,7]{2,1,3,0:T(8,128)} %get-tuple-element.234, f32[4,7,256]{2,1,0:T(8,128)S(1)} %select_maximum_fusion.2, pred[256,512]{0,1:T(8,128)(4,1)S(1)} %compare_and_fusion.2, ...), kind=kOutput, calls=%fused_computation.11.clone.1 | convolution fusion | flops 956956672 | bytes 22732800 | tf_op jit(solution)/shard_map/while/body/eval_jaxpr/ghrn,ngo->ghro/dot_general | solution.py:90
  383.0 1.9 copy-done.2
  387.8 6.5 %fusion.43 = (f32[4,7,256]{2,1,0:T(8,128)S(1)}, f32[4,512,256,7]{2,1,3,0:T(8,128)}) fusion(pred[256,512]{0,1:T(8,128)(4,1)S(1)} %compare_and_fusion.2, bf16[512,4,128,1]{0,2,3,1:T(8,128)(2,1)S(1)} %bitcast.80, bf16[256,4,7,128]{3,0,2,1:T(8,128)(2,1)S(1)} %get-tuple-element.270), kind=kOutput, calls=%fused_computation.3.clone.1 | convolution fusion | flops 950526976 | bytes 17199104 | tf_op jit(solution)/shard_map/while/body/eval_jaxpr/rgho,ngo->ghrn/dot_general | solution.py:80
  394.4 8.3 %fusion.44 = f32[4,7,256]{2,1,0:T(8,128)S(1)} fusion(f32[4,512,256,7]{2,1,3,0:T(8,128)} %get-tuple-element.234, f32[4,7,256]{2,1,0:T(8,128)S(1)} %select_maximum_fusion.2, pred[256,512]{0,1:T(8,128)(4,1)S(1)} %compare_and_fusion.2), kind=kLoop, calls=%fused_computation.7.clone.1 | loop fusion | flops 14672896 | bytes 14868480 | tf_op jit(solution)/shard_map/while/body/eval_jaxpr/reduce_sum | solution.py:89
  402.7 8.0 %fusion.46 = f32[4,7,256,128]{3,2,1,0:T(8,128)S(1)} fusion(f32[4,7,256,128]{3,2,1,0:T(8,128)S(1)} %copy-done.1, bf16[512,4,128,1]{0,2,3,1:T(8,128)(2,1)S(1)} %bitcast.82, f32[4,512,256,7]{2,1,3,0:T(8,128)} %get-tuple-element.234, f32[4,7,256]{2,1,0:T(8,128)S(1)} %select_maximum_fusion.2, pred[256,512]{0,1:T(8,128)(4,1)S(1)} %compare_and_fusion.2, ...), kind=kOutput, calls=%fused_computation.11.clone.1 | convolution fusion | flops 956956672 | bytes 22732800 | tf_op jit(solution)/shard_map/while/body/eval_jaxpr/ghrn,ngo->ghro/dot_general | solution.py:90
  410.8 1.9 copy-done.2
  415.6 6.5 %fusion.43 = (f32[4,7,256]{2,1,0:T(8,128)S(1)}, f32[4,512,256,7]{2,1,3,0:T(8,128)}) fusion(pred[256,512]{0,1:T(8,128)(4,1)S(1)} %compare_and_fusion.2, bf16[512,4,128,1]{0,2,3,1:T(8,128)(2,1)S(1)} %bitcast.80, bf16[256,4,7,128]{3,0,2,1:T(8,128)(2,1)S(1)} %get-tuple-element.270), kind=kOutput, calls=%fused_computation.3.clone.1 | convolution fusion | flops 950526976 | bytes 17199104 | tf_op jit(solution)/shard_map/while/body/eval_jaxpr/rgho,ngo->ghrn/dot_general | solution.py:80
  422.1 8.3 %fusion.44 = f32[4,7,256]{2,1,0:T(8,128)S(1)} fusion(f32[4,512,256,7]{2,1,3,0:T(8,128)} %get-tuple-element.234, f32[4,7,256]{2,1,0:T(8,128)S(1)} %select_maximum_fusion.2, pred[256,512]{0,1:T(8,128)(4,1)S(1)} %compare_and_fusion.2), kind=kLoop, calls=%fused_computation.7.clone.1 | loop fusion | flops 14672896 | bytes 14868480 | tf_op jit(solution)/shard_map/while/body/eval_jaxpr/reduce_sum | solution.py:89
  430.5 8.0 %fusion.46 = f32[4,7,256,128]{3,2,1,0:T(8,128)S(1)} fusion(f32[4,7,256,128]{3,2,1,0:T(8,128)S(1)} %copy-done.1, bf16[512,4,128,1]{0,2,3,1:T(8,128)(2,1)S(1)} %bitcast.82, f32[4,512,256,7]{2,1,3,0:T(8,128)} %get-tuple-element.234, f32[4,7,256]{2,1,0:T(8,128)S(1)} %select_maximum_fusion.2, pred[256,512]{0,1:T(8,128)(4,1)S(1)} %compare_and_fusion.2, ...), kind=kOutput, calls=%fused_computation.11.clone.1 | convolution fusion | flops 956956672 | bytes 22732800 | tf_op jit(solution)/shard_map/while/body/eval_jaxpr/ghrn,ngo->ghro/dot_general | solution.py:90
  438.5 1.9 copy-done.2
  443.3 6.5 %fusion.43 = (f32[4,7,256]{2,1,0:T(8,128)S(1)}, f32[4,512,256,7]{2,1,3,0:T(8,128)}) fusion(pred[256,512]{0,1:T(8,128)(4,1)S(1)} %compare_and_fusion.2, bf16[512,4,128,1]{0,2,3,1:T(8,128)(2,1)S(1)} %bitcast.80, bf16[256,4,7,128]{3,0,2,1:T(8,128)(2,1)S(1)} %get-tuple-element.270), kind=kOutput, calls=%fused_computation.3.clone.1 | convolution fusion | flops 950526976 | bytes 17199104 | tf_op jit(solution)/shard_map/while/body/eval_jaxpr/rgho,ngo->ghrn/dot_general | solution.py:80
  449.9 8.3 %fusion.44 = f32[4,7,256]{2,1,0:T(8,128)S(1)} fusion(f32[4,512,256,7]{2,1,3,0:T(8,128)} %get-tuple-element.234, f32[4,7,256]{2,1,0:T(8,128)S(1)} %select_maximum_fusion.2, pred[256,512]{0,1:T(8,128)(4,1)S(1)} %compare_and_fusion.2), kind=kLoop, calls=%fused_computation.7.clone.1 | loop fusion | flops 14672896 | bytes 14868480 | tf_op jit(solution)/shard_map/while/body/eval_jaxpr/reduce_sum | solution.py:89
  458.2 8.0 %fusion.46 = f32[4,7,256,128]{3,2,1,0:T(8,128)S(1)} fusion(f32[4,7,256,128]{3,2,1,0:T(8,128)S(1)} %copy-done.1, bf16[512,4,128,1]{0,2,3,1:T(8,128)(2,1)S(1)} %bitcast.82, f32[4,512,256,7]{2,1,3,0:T(8,128)} %get-tuple-element.234, f32[4,7,256]{2,1,0:T(8,128)S(1)} %select_maximum_fusion.2, pred[256,512]{0,1:T(8,128)(4,1)S(1)} %compare_and_fusion.2, ...), kind=kOutput, calls=%fused_computation.11.clone.1 | convolution fusion | flops 956956672 | bytes 22732800 | tf_op jit(solution)/shard_map/while/body/eval_jaxpr/ghrn,ngo->ghro/dot_general | solution.py:90
  466.3 1.9 copy-done.2
  471.1 6.5 %fusion.43 = (f32[4,7,256]{2,1,0:T(8,128)S(1)}, f32[4,512,256,7]{2,1,3,0:T(8,128)}) fusion(pred[256,512]{0,1:T(8,128)(4,1)S(1)} %compare_and_fusion.2, bf16[512,4,128,1]{0,2,3,1:T(8,128)(2,1)S(1)} %bitcast.80, bf16[256,4,7,128]{3,0,2,1:T(8,128)(2,1)S(1)} %get-tuple-element.270), kind=kOutput, calls=%fused_computation.3.clone.1 | convolution fusion | flops 950526976 | bytes 17199104 | tf_op jit(solution)/shard_map/while/body/eval_jaxpr/rgho,ngo->ghrn/dot_general | solution.py:80
  477.6 8.3 %fusion.44 = f32[4,7,256]{2,1,0:T(8,128)S(1)} fusion(f32[4,512,256,7]{2,1,3,0:T(8,128)} %get-tuple-element.234, f32[4,7,256]{2,1,0:T(8,128)S(1)} %select_maximum_fusion.2, pred[256,512]{0,1:T(8,128)(4,1)S(1)} %compare_and_fusion.2), kind=kLoop, calls=%fused_computation.7.clone.1 | loop fusion | flops 14672896 | bytes 14868480 | tf_op jit(solution)/shard_map/while/body/eval_jaxpr/reduce_sum | solution.py:89
  486.0 8.0 %fusion.46 = f32[4,7,256,128]{3,2,1,0:T(8,128)S(1)} fusion(f32[4,7,256,128]{3,2,1,0:T(8,128)S(1)} %copy-done.1, bf16[512,4,128,1]{0,2,3,1:T(8,128)(2,1)S(1)} %bitcast.82, f32[4,512,256,7]{2,1,3,0:T(8,128)} %get-tuple-element.234, f32[4,7,256]{2,1,0:T(8,128)S(1)} %select_maximum_fusion.2, pred[256,512]{0,1:T(8,128)(4,1)S(1)} %compare_and_fusion.2, ...), kind=kOutput, calls=%fused_computation.11.clone.1 | convolution fusion | flops 956956672 | bytes 22732800 | tf_op jit(solution)/shard_map/while/body/eval_jaxpr/ghrn,ngo->ghro/dot_general | solution.py:90
  494.0 1.9 copy-done.2
  498.8 6.5 %fusion.43 = (f32[4,7,256]{2,1,0:T(8,128)S(1)}, f32[4,512,256,7]{2,1,3,0:T(8,128)}) fusion(pred[256,512]{0,1:T(8,128)(4,1)S(1)} %compare_and_fusion.2, bf16[512,4,128,1]{0,2,3,1:T(8,128)(2,1)S(1)} %bitcast.80, bf16[256,4,7,128]{3,0,2,1:T(8,128)(2,1)S(1)} %get-tuple-element.270), kind=kOutput, calls=%fused_computation.3.clone.1 | convolution fusion | flops 950526976 | bytes 17199104 | tf_op jit(solution)/shard_map/while/body/eval_jaxpr/rgho,ngo->ghrn/dot_general | solution.py:80
  505.4 8.3 %fusion.44 = f32[4,7,256]{2,1,0:T(8,128)S(1)} fusion(f32[4,512,256,7]{2,1,3,0:T(8,128)} %get-tuple-element.234, f32[4,7,256]{2,1,0:T(8,128)S(1)} %select_maximum_fusion.2, pred[256,512]{0,1:T(8,128)(4,1)S(1)} %compare_and_fusion.2), kind=kLoop, calls=%fused_computation.7.clone.1 | loop fusion | flops 14672896 | bytes 14868480 | tf_op jit(solution)/shard_map/while/body/eval_jaxpr/reduce_sum | solution.py:89
  513.7 8.0 %fusion.46 = f32[4,7,256,128]{3,2,1,0:T(8,128)S(1)} fusion(f32[4,7,256,128]{3,2,1,0:T(8,128)S(1)} %copy-done.1, bf16[512,4,128,1]{0,2,3,1:T(8,128)(2,1)S(1)} %bitcast.82, f32[4,512,256,7]{2,1,3,0:T(8,128)} %get-tuple-element.234, f32[4,7,256]{2,1,0:T(8,128)S(1)} %select_maximum_fusion.2, pred[256,512]{0,1:T(8,128)(4,1)S(1)} %compare_and_fusion.2, ...), kind=kOutput, calls=%fused_computation.11.clone.1 | convolution fusion | flops 956956672 | bytes 22732800 | tf_op jit(solution)/shard_map/while/body/eval_jaxpr/ghrn,ngo->ghro/dot_general | solution.py:90
  521.8 1.9 copy-done.2
  526.6 6.5 %fusion.43 = (f32[4,7,256]{2,1,0:T(8,128)S(1)}, f32[4,512,256,7]{2,1,3,0:T(8,128)}) fusion(pred[256,512]{0,1:T(8,128)(4,1)S(1)} %compare_and_fusion.2, bf16[512,4,128,1]{0,2,3,1:T(8,128)(2,1)S(1)} %bitcast.80, bf16[256,4,7,128]{3,0,2,1:T(8,128)(2,1)S(1)} %get-tuple-element.270), kind=kOutput, calls=%fused_computation.3.clone.1 | convolution fusion | flops 950526976 | bytes 17199104 | tf_op jit(solution)/shard_map/while/body/eval_jaxpr/rgho,ngo->ghrn/dot_general | solution.py:80
  533.1 8.3 %fusion.44 = f32[4,7,256]{2,1,0:T(8,128)S(1)} fusion(f32[4,512,256,7]{2,1,3,0:T(8,128)} %get-tuple-element.234, f32[4,7,256]{2,1,0:T(8,128)S(1)} %select_maximum_fusion.2, pred[256,512]{0,1:T(8,128)(4,1)S(1)} %compare_and_fusion.2), kind=kLoop, calls=%fused_computation.7.clone.1 | loop fusion | flops 14672896 | bytes 14868480 | tf_op jit(solution)/shard_map/while/body/eval_jaxpr/reduce_sum | solution.py:89
  541.5 8.0 %fusion.46 = f32[4,7,256,128]{3,2,1,0:T(8,128)S(1)} fusion(f32[4,7,256,128]{3,2,1,0:T(8,128)S(1)} %copy-done.1, bf16[512,4,128,1]{0,2,3,1:T(8,128)(2,1)S(1)} %bitcast.82, f32[4,512,256,7]{2,1,3,0:T(8,128)} %get-tuple-element.234, f32[4,7,256]{2,1,0:T(8,128)S(1)} %select_maximum_fusion.2, pred[256,512]{0,1:T(8,128)(4,1)S(1)} %compare_and_fusion.2, ...), kind=kOutput, calls=%fused_computation.11.clone.1 | convolution fusion | flops 956956672 | bytes 22732800 | tf_op jit(solution)/shard_map/while/body/eval_jaxpr/ghrn,ngo->ghro/dot_general | solution.py:90
  549.5 1.9 copy-done.2
  554.3 6.5 %fusion.43 = (f32[4,7,256]{2,1,0:T(8,128)S(1)}, f32[4,512,256,7]{2,1,3,0:T(8,128)}) fusion(pred[256,512]{0,1:T(8,128)(4,1)S(1)} %compare_and_fusion.2, bf16[512,4,128,1]{0,2,3,1:T(8,128)(2,1)S(1)} %bitcast.80, bf16[256,4,7,128]{3,0,2,1:T(8,128)(2,1)S(1)} %get-tuple-element.270), kind=kOutput, calls=%fused_computation.3.clone.1 | convolution fusion | flops 950526976 | bytes 17199104 | tf_op jit(solution)/shard_map/while/body/eval_jaxpr/rgho,ngo->ghrn/dot_general | solution.py:80
  560.9 8.3 %fusion.44 = f32[4,7,256]{2,1,0:T(8,128)S(1)} fusion(f32[4,512,256,7]{2,1,3,0:T(8,128)} %get-tuple-element.234, f32[4,7,256]{2,1,0:T(8,128)S(1)} %select_maximum_fusion.2, pred[256,512]{0,1:T(8,128)(4,1)S(1)} %compare_and_fusion.2), kind=kLoop, calls=%fused_computation.7.clone.1 | loop fusion | flops 14672896 | bytes 14868480 | tf_op jit(solution)/shard_map/while/body/eval_jaxpr/reduce_sum | solution.py:89
  569.2 8.0 %fusion.46 = f32[4,7,256,128]{3,2,1,0:T(8,128)S(1)} fusion(f32[4,7,256,128]{3,2,1,0:T(8,128)S(1)} %copy-done.1, bf16[512,4,128,1]{0,2,3,1:T(8,128)(2,1)S(1)} %bitcast.82, f32[4,512,256,7]{2,1,3,0:T(8,128)} %get-tuple-element.234, f32[4,7,256]{2,1,0:T(8,128)S(1)} %select_maximum_fusion.2, pred[256,512]{0,1:T(8,128)(4,1)S(1)} %compare_and_fusion.2, ...), kind=kOutput, calls=%fused_computation.11.clone.1 | convolution fusion | flops 956956672 | bytes 22732800 | tf_op jit(solution)/shard_map/while/body/eval_jaxpr/ghrn,ngo->ghro/dot_general | solution.py:90
  579.1 4.6 copy.38
  583.7 2.5 divide_convert_fusion
  586.2 2.6 copy.39
  (137 shorter events, 34.8 us)
Async XLA Ops:
  7.2 30.8 %all-gather.9.cloned.1.call-start = ((), (), s32[]{:S(2)}) async-start(), calls=%async_computation.3 | async-start | bytes 2654208 | tf_op jit(solution)/shard_map/all_gather | solution.py:43
  7.9 208.7 %all-gather.5.cloned.1.call-start = ((), (), s32[]{:S(2)}) async-start(), calls=%async_computation.1 | async-start | bytes 31195136 | tf_op jit(solution)/shard_map/all_gather | solution.py:40
  231.3 7.2 %copy-start.3 = (s32[1,4]{1,0:T(1,128)S(1)}, s32[1,4]{1,0:T(1,128)}, u32[]{:S(2)}) copy-start(s32[1,4]{1,0:T(1,128)} %param.8) | copy-start | bytes 52
  233.0 40.5 %all-to-all-start = ((bf16[16,256,288]{1,2,0:T(8,128)(2,1)}), bf16[16,256,288]{1,2,0:T(8,128)(2,1)S(1)}, u32[]{:S(2)}, u32[]{:S(2)}) async-start(bf16[16,256,288]{1,2,0:T(8,128)(2,1)} %bitcast.85), calls=%async_computation | async-start | bytes 4718592 | tf_op jit(solution)/shard_map/all_to_all | solution.py:49
  238.2 111.5 %all-gather.7.cloned.1.call-start = ((), (), s32[]{:S(2)}) async-start(), calls=%async_computation.2 | async-start | bytes 8912896 | tf_op jit(solution)/shard_map/all_gather | solution.py:106
  274.5 1.4 copy-start
  366.6 8.4 %copy-start.1 = (f32[4,7,256,128]{3,2,1,0:T(8,128)S(1)}, f32[4,7,256,128]{3,2,1,0:T(8,128)}, u32[]{:S(2)}) copy-start(f32[4,7,256,128]{3,2,1,0:T(8,128)} %get-tuple-element.253) | copy-start | bytes 11010052 | tf_op jit(solution)/shard_map/while
  383.0 1.9 copy-start.2
  394.4 8.4 %copy-start.1 = (f32[4,7,256,128]{3,2,1,0:T(8,128)S(1)}, f32[4,7,256,128]{3,2,1,0:T(8,128)}, u32[]{:S(2)}) copy-start(f32[4,7,256,128]{3,2,1,0:T(8,128)} %get-tuple-element.253) | copy-start | bytes 11010052 | tf_op jit(solution)/shard_map/while
  410.8 1.9 copy-start.2
  422.1 8.4 %copy-start.1 = (f32[4,7,256,128]{3,2,1,0:T(8,128)S(1)}, f32[4,7,256,128]{3,2,1,0:T(8,128)}, u32[]{:S(2)}) copy-start(f32[4,7,256,128]{3,2,1,0:T(8,128)} %get-tuple-element.253) | copy-start | bytes 11010052 | tf_op jit(solution)/shard_map/while
  438.5 1.9 copy-start.2
  449.9 8.4 %copy-start.1 = (f32[4,7,256,128]{3,2,1,0:T(8,128)S(1)}, f32[4,7,256,128]{3,2,1,0:T(8,128)}, u32[]{:S(2)}) copy-start(f32[4,7,256,128]{3,2,1,0:T(8,128)} %get-tuple-element.253) | copy-start | bytes 11010052 | tf_op jit(solution)/shard_map/while
  466.3 1.9 copy-start.2
  477.6 8.4 %copy-start.1 = (f32[4,7,256,128]{3,2,1,0:T(8,128)S(1)}, f32[4,7,256,128]{3,2,1,0:T(8,128)}, u32[]{:S(2)}) copy-start(f32[4,7,256,128]{3,2,1,0:T(8,128)} %get-tuple-element.253) | copy-start | bytes 11010052 | tf_op jit(solution)/shard_map/while
  494.0 1.9 copy-start.2
  505.4 8.4 %copy-start.1 = (f32[4,7,256,128]{3,2,1,0:T(8,128)S(1)}, f32[4,7,256,128]{3,2,1,0:T(8,128)}, u32[]{:S(2)}) copy-start(f32[4,7,256,128]{3,2,1,0:T(8,128)} %get-tuple-element.253) | copy-start | bytes 11010052 | tf_op jit(solution)/shard_map/while
  521.8 1.9 copy-start.2
  533.1 8.4 %copy-start.1 = (f32[4,7,256,128]{3,2,1,0:T(8,128)S(1)}, f32[4,7,256,128]{3,2,1,0:T(8,128)}, u32[]{:S(2)}) copy-start(f32[4,7,256,128]{3,2,1,0:T(8,128)} %get-tuple-element.253) | copy-start | bytes 11010052 | tf_op jit(solution)/shard_map/while
  549.5 1.9 copy-start.2
  560.9 8.4 %copy-start.1 = (f32[4,7,256,128]{3,2,1,0:T(8,128)S(1)}, f32[4,7,256,128]{3,2,1,0:T(8,128)}, u32[]{:S(2)}) copy-start(f32[4,7,256,128]{3,2,1,0:T(8,128)} %get-tuple-element.253) | copy-start | bytes 11010052 | tf_op jit(solution)/shard_map/while
  577.3 1.9 copy-start.2
Sparse Core Ops, SparseCore 0:
  9.7 28.2 all-gather.8
  40.7 175.8 all-gather.4
  274.6 75.0 all-gather.6
where the time goes:
time: 597 us; the launch traced here: 595 us
  waiting for transfers between devices  297 us (50%)
  matrix products  131 us (22%)
  other arithmetic  87.5 us (15%)
  local copies, waits for them, and re-layouts  59.6 us (10%)
  between operations  13.9 us (2%)
    all_gather x1, waiting for transfers between devices, project_joined(): grouped = lax.all_gather(normed, 'gy', axis=0, tiled=True)  172 us
    reduce_sum x8, other arithmetic, attend(): total = total * shrink + jnp.sum(weights, axis=3)  66.5 us
    all_gather x1, waiting for transfers between devices, on_device(): piece = lax.all_gather(kv_rows, 'gy', axis=0, tiled=True)  65.9 us
    dot_general x8, matrix products, attend(): jnp.einsum('ghrn,ngo->ghro', weights.astype(jnp.bfloat16), value_part, pr...  64.3 us
    dot_general x8, matrix products, attend(): jnp.einsum('rgho,ngo->ghrn', queries, key_part, preferred_element_type=jn...  52.3 us
    all_to_all x1, waiting for transfers between devices, project_joined(): lax.all_to_all(block_out, 'gy', split_axis=0, concat_axis=1, tiled=True)  34.4 us
    all_gather x1, waiting for transfers between devices, project_joined(): lax.all_gather(weight, 'gx', axis=0, tiled=True)  24 us
    while x40, local copies, waits for them, and re-layouts  15 us
  transfers between devices with their start and end apart: 4, of which 4 were waited for; matrix products, arithmetic and copies ran while one was open for 4% of the time, Pallas kernels for 0%

commit v1 on v0

--- a/solution.py
+++ b/solution.py
@@ -37,7 +37,9 @@
 
 
 def project_joined(normed, weight, bias):
-    grouped = lax.all_gather(normed, "gy", axis=0, tiled=True)
+    grouped = jnp.concatenate(
+        lax.all_to_all(jnp.stack([normed] * lax.axis_size("gy")), "gy", 0, 0), axis=0
+    )
     summed = jnp.dot(
         grouped,
         lax.all_gather(weight, "gx", axis=0, tiled=True),

time: 597 us -> 845 us (1.42)
  waiting for transfers between devices: 297 us -> 531 us
  local copies, waits for them, and re-layouts: 59.6 us -> 69.7 us
    all_to_all x0 -> x1, waiting for transfers between devices: none -> 402 us  [project_joined(): lax.all_to_all(jnp.stack([normed] * lax.axis_size('gy')), 'gy', 0, 0)]
    all_gather x1 -> x0, waiting for transfers between devices: 172 us -> none  [project_joined(): grouped = lax.all_gather(normed, 'gy', axis=0, tiled=True)]
    another operation x0 -> x1, local copies, waits for them, and re-layouts: none -> 10.1 us  [project_joined(): jnp.stack([normed] * lax.axis_size('gy'))]
  transfers between devices with their start and end apart: 4 -> 4, of which waited for: 4 -> 4; matrix products, arithmetic and copies ran while one was open for 4% -> 2% of each run, Pallas kernels for 0% -> 0%
where the time goes in v1:
time: 845 us; the launch traced here: 844 us
  waiting for transfers between devices  531 us (63%)
  matrix products  132 us (16%)
  other arithmetic  86.2 us (10%)
  local copies, waits for them, and re-layouts  69.7 us (8%)
  between operations  14.2 us (2%)
  starting transfers between devices  11.2 us (1%)
    all_to_all x1, waiting for transfers between devices, project_joined(): lax.all_to_all(jnp.stack([normed] * lax.axis_size('gy')), 'gy', 0, 0)  402 us
    all_gather x1, waiting for transfers between devices, on_device(): piece = lax.all_gather(kv_rows, 'gy', axis=0, tiled=True)  66.5 us
    reduce_sum x8, other arithmetic, attend(): total = total * shrink + jnp.sum(weights, axis=3)  66.5 us
    dot_general x8, matrix products, attend(): jnp.einsum('ghrn,ngo->ghro', weights.astype(jnp.bfloat16), value_part, pr...  64.3 us
    dot_general x8, matrix products, attend(): jnp.einsum('rgho,ngo->ghrn', queries, key_part, preferred_element_type=jn...  52.7 us
    all_to_all x1, waiting for transfers between devices, project_joined(): lax.all_to_all(block_out, 'gy', split_axis=0, concat_axis=1, tiled=True)  32.5 us
    all_gather x1, waiting for transfers between devices, project_joined(): lax.all_gather(weight, 'gx', axis=0, tiled=True)  29.3 us
  transfers between devices with their start and end apart: 4, of which 4 were waited for; matrix products, arithmetic and copies ran while one was open for 2% of the time, Pallas kernels for 0%

profile of v1, /device:TPU:0, one launch (start us, length us, event | category | flops | bytes accessed | tf_op | source)
XLA Modules:
  0.0 844.1 jit_solution(1912717674778952443)
XLA Ops:
  7.2 1.9 fusion.17
  9.1 2.0 fusion.19
  11.1 10.1 %stack.2 = bf16[16,256,3584]{2,1,0:T(8,128)(2,1)} broadcast(bf16[256,3584]{1,0:T(8,128)(2,1)S(1)} %fusion.19), dimensions={1,2} | broadcast | bytes 31195136 | tf_op jit(solution)/shard_map/stack | solution.py:41
  21.2 7.2 all-to-all-start
  29.9 29.3 %all-gather.6.cloned.1.call-done = bf16[8,448,288]{1,2,0:T(8,128)(2,1)} async-done(((bf16[1,448,288]{1,2,0:T(8,128)(2,1)}), bf16[8,448,288]{1,2,0:T(8,128)(2,1)}) %all-gather.6.cloned.1.call-update) | async-done | bytes 2064400 | tf_op jit(solution)/shard_map/all_gather | solution.py:45
  59.3 3.0 copy.34
  62.2 3.6 reshape.178
  65.8 401.6 %all-to-all-done = bf16[16,256,3584]{2,1,0:T(8,128)(2,1)} async-done(((bf16[16,256,3584]{2,1,0:T(8,128)(2,1)}), bf16[16,256,3584]{2,1,0:T(8,128)(2,1)}, u32[]{:S(2)}, u32[]{:S(2)}) %all-to-all-start) | async-done | bytes 29360160 | tf_op jit(solution)/shard_map/all_to_all | solution.py:41
  467.4 14.7 %fusion.16 = bf16[4096,288]{0,1:T(8,128)(2,1)S(1)} fusion(bf16[4096,3584]{1,0:T(8,128)(2,1)} %bitcast.2, bf16[3584,288]{0,1:T(8,128)(2,1)} %reshape.178, f32[288]{0:T(512)S(1)} %dynamic_slice.11), kind=kOutput, calls=%fused_computation.25 | convolution fusion | flops 8458076160 | bytes 33784960 | tf_op jit(solution)/shard_map/dot_general | solution.py:43
  483.7 3.7 all-to-all-start.1
  488.3 32.5 %all-to-all-done.1 = bf16[16,256,288]{1,2,0:T(8,128)(2,1)S(1)} async-done(((bf16[16,256,288]{1,2,0:T(8,128)(2,1)}), bf16[16,256,288]{1,2,0:T(8,128)(2,1)S(1)}, u32[]{:S(2)}, u32[]{:S(2)}) %all-to-all-start.1) | async-done | bytes 2359328 | tf_op jit(solution)/shard_map/all_to_all | solution.py:51
  524.4 1.9 convert.19
  528.3 2.9 copy.37
  531.2 66.5 %all-gather.4.cloned.1.call-done = bf16[4096,1024]{0,1:T(8,128)(2,1)} async-done(((bf16[256,1024]{0,1:T(8,128)(2,1)}), bf16[4096,1024]{0,1:T(8,128)(2,1)}) %all-gather.4.cloned.1.call-update) | async-done | bytes 8388624 | tf_op jit(solution)/shard_map/all_gather | solution.py:108
  597.7 7.5 copy.52
  605.2 222.4 %while.15 = (s32[]{:T(128)}, f32[4,7,256]{2,1,0:T(8,128)S(1)}, f32[4,7,256]{2,1,0:T(8,128)S(1)}, f32[4,7,256,128]{3,2,1,0:T(8,128)}, s32[256]{0:T(256)S(1)}, /*i...) while((s32[]{:T(128)}, f32[4,7,256]{2,1,0:T(8,128)S(1)}, ...), condition=%wide.region_8.9_spmd.clone, body=%wide.region_4.8_spmd.clone.sunk | while | flops 1922606336 | bytes 88814816 | solution.py:117
  608.1 6.6 fusion.43
  614.7 8.3 fusion.44
  623.0 8.0 fusion.46
  631.1 1.9 copy-done.2
  635.9 6.6 fusion.43
  642.5 8.3 fusion.44
  650.9 8.0 fusion.46
  658.9 1.9 copy-done.2
  663.7 6.6 fusion.43
  670.3 8.3 fusion.44
  678.6 8.0 fusion.46
  686.7 1.9 copy-done.2
  691.5 6.6 fusion.43
  698.1 8.3 fusion.44
  706.4 8.0 fusion.46
  714.5 1.9 copy-done.2
  719.3 6.6 fusion.43
  725.9 8.3 fusion.44
  734.2 8.0 fusion.46
  742.3 1.9 copy-done.2
  747.1 6.6 fusion.43
  753.7 8.3 fusion.44
  762.0 8.0 fusion.46
  774.9 6.6 fusion.43
  781.5 8.3 fusion.44
  789.8 8.0 fusion.46
  802.7 6.6 fusion.43
  809.3 8.3 fusion.44
  817.6 8.0 fusion.46
  827.6 4.6 copy.38
  832.2 2.5 divide_convert_fusion
  834.7 2.6 copy.39
  (137 shorter events, 38.5 us)
Async XLA Ops:
  21.2 446.2 %all-to-all-start = ((bf16[16,256,3584]{2,1,0:T(8,128)(2,1)}), bf16[16,256,3584]{2,1,0:T(8,128)(2,1)}, u32[]{:S(2)}, u32[]{:S(2)}) async-start(bf16[16,256,3584]{2,1,0:T(8,128)(2,1)} %stack.2), calls=%async_computation | async-start | bytes 58720256 | tf_op jit(solution)/shard_map/all_to_all | solution.py:41
  28.4 30.8 %all-gather.6.cloned.1.call-start = ((), (), s32[]{:S(2)}) async-start(), calls=%async_computation.3 | async-start | bytes 2654208 | tf_op jit(solution)/shard_map/all_gather | solution.py:45
  482.1 5.6 copy-start.3
  483.7 37.1 %all-to-all-start.1 = ((bf16[16,256,288]{1,2,0:T(8,128)(2,1)}), bf16[16,256,288]{1,2,0:T(8,128)(2,1)S(1)}, u32[]{:S(2)}, u32[]{:S(2)}) async-start(bf16[16,256,288]{1,2,0:T(8,128)(2,1)} %bitcast.86), calls=%async_computation.1 | async-start | bytes 4718592 | tf_op jit(solution)/shard_map/all_to_all | solution.py:51
  487.5 110.2 %all-gather.4.cloned.1.call-start = ((), (), s32[]{:S(2)}) async-start(), calls=%async_computation.2 | async-start | bytes 8912896 | tf_op jit(solution)/shard_map/all_gather | solution.py:108
  521.9 1.4 copy-start
  614.7 8.4 copy-start.1
  631.1 1.9 copy-start.2
  642.5 8.4 copy-start.1
  658.9 1.9 copy-start.2
  670.3 8.4 copy-start.1
  686.7 1.9 copy-start.2
  698.1 8.4 copy-start.1
  714.5 1.9 copy-start.2
  725.9 8.4 copy-start.1
  742.3 1.9 copy-start.2
  753.7 8.4 copy-start.1
  770.1 1.9 copy-start.2
  781.5 8.4 copy-start.1
  797.9 1.9 copy-start.2
  809.3 8.4 copy-start.1
  825.7 1.9 copy-start.2
Sparse Core Ops, SparseCore 0:
  30.9 28.3 all-gather.5
  522.1 75.5 all-gather.3
